TPU v7x, 32 devices: a whole 2x2x4 slice. The times are simulated.
32 devices in a mesh: dp: 8 (over z, y), mp: 4 (over x, core).
Axes of the slice: x: 2, y: 2, z: 4, core: 2. Of those that a mesh axis runs over, the one named last changes fastest.
Arguments:
- tokens: bfloat16 [32, 512, 768], P('dp'), may hold values from -6 to 6
- prev_logits: bfloat16 [32, 12, 512, 512], P('dp', 'mp'), may hold values from -6 to 6
- segment_ids: int32 [32, 512], P('dp'), may hold values from -1 to 3, as said below
- w_qkv: bfloat16 [768, 3, 768], P(None, None, 'mp'), may hold values from -0.21875 to 0.21875
- bias_qv: bfloat16 [2, 768], P(None, 'mp'), may hold values from -3 to 3
- w_out: bfloat16 [768, 768], P('mp'), may hold values from -1.5 to 1.5
- b_out: bfloat16 [768], replicated, may hold values from -3 to 3
- gain_one: bfloat16 [768], replicated, may hold values from 0.25 to 1.75
- shift_one: bfloat16 [768], replicated, may hold values from -3 to 3
- w_in: bfloat16 [768, 3072], P(None, 'mp'), may hold values from -0.21875 to 0.21875
- b_in: bfloat16 [3072], P('mp'), may hold values from -3 to 3
- w_back: bfloat16 [3072, 768], P('mp'), may hold values from -0.109375 to 0.109375
- b_back: bfloat16 [768], replicated, may hold values from -3 to 3
- gain_two: bfloat16 [768], replicated, may hold values from 0.25 to 1.75
- shift_two: bfloat16 [768], replicated, may hold values from -3 to 3
- cotangent: bfloat16 [32, 512, 768], P('dp'), may hold values from -6 to 6
Outputs:
- output: bfloat16 [32, 512, 768], P('dp')
- raw_logits: bfloat16 [32, 12, 512, 512], P('dp', 'mp')
- grad_tokens: bfloat16 [32, 512, 768], P('dp')
- grad_prev: bfloat16 [32, 12, 512, 512], P('dp', 'mp')
- grad_w_qkv: float32 [768, 3, 768], P(None, None, 'mp')
- grad_bias_qv: float32 [2, 768], P(None, 'mp')
- grad_w_out: float32 [768, 768], P('mp')
- grad_b_out: float32 [768], replicated
- grad_gain_one: float32 [768], replicated
- grad_shift_one: float32 [768], replicated
- grad_w_in: float32 [768, 3072], P(None, 'mp')
- grad_b_in: float32 [3072], P('mp')
- grad_w_back: float32 [3072, 768], P('mp')
- grad_b_back: float32 [768], replicated
- grad_gain_two: float32 [768], replicated
- grad_shift_two: float32 [768], replicated
Inputs may be any that keep to these rules, and one draw needn't show every extreme that they name: `segment_ids`: each row holds 4 documents numbered 0 to 3 in order, each a run of consecutive slots, followed by one or more padding slots marked -1 at the row's end.
All inputs are finite; a program needn't handle non-finite values.
Results may differ from a plain program's by a relative error of at most 0.014.
The roundings to bfloat16 on the way count: a program that leaves them out, or rounds other values in their place, can miss the bound.
Values sent between devices are 32-bit elements; how exact they have to be, the bound alone decides.
No kernel may reach another device: no remote copies, remote signals or barrier semaphores. Data moves between devices by JAX's collectives and lax.ppermute only.
A program may use at most 192 MiB of HBM per device.

v0:
```python
import jax
import jax.numpy as jnp
from jax import lax
from jax.sharding import PartitionSpec as P


def normalize(hidden, gain, shift):
    average = jnp.mean(hidden, axis=-1, keepdims=True)
    centred = hidden - average
    spread = jnp.mean(centred * centred, axis=-1, keepdims=True)
    return centred * lax.rsqrt(spread + 1e-05) * gain + shift


def gelu_exact(value):
    return jax.nn.gelu(value, approximate=False)


def mask_for(segment):
    allowed = (segment[:, None] == segment[None, :]) & (segment[None, :] >= 0)
    return jnp.where(allowed, 0.0, -10000.0).astype(jnp.float32)


def row_scores(queries, key_rows, previous, segment):
    product = jnp.einsum("qhe,khe->hqk", queries, key_rows, preferred_element_type=jnp.float32)
    logits = product * 0.125 + previous.astype(jnp.float32)
    return (logits, logits + mask_for(segment)[None])


def attend_row(items):
    queries, key_rows, values, previous, segment = items
    logits, scores = row_scores(queries, key_rows, previous, segment)
    largest = jnp.max(scores, axis=-1, keepdims=True)
    total = jnp.sum(jnp.exp(scores - largest), axis=-1, keepdims=True)
    log_total = largest + jnp.log(total)
    weights = jnp.exp(scores - log_total).astype(jnp.bfloat16)
    context = jnp.einsum("hqk,khe->qhe", weights, values, preferred_element_type=jnp.float32)
    return (logits.astype(jnp.bfloat16), log_total, context.astype(jnp.bfloat16))


def attend_back_row(items):
    queries, key_rows, values, previous, segment, log_total, grad_context = items
    unused, scores = row_scores(queries, key_rows, previous, segment)
    weights = jnp.exp(scores - log_total)
    grad_weights = jnp.einsum(
        "qhe,khe->hqk", grad_context, values, preferred_element_type=jnp.float32
    )
    grad_values = jnp.einsum(
        "hqk,qhe->khe",
        weights.astype(jnp.bfloat16),
        grad_context,
        preferred_element_type=jnp.float32,
    )
    grad_scores = weights * (grad_weights - jnp.sum(weights * grad_weights, axis=-1, keepdims=True))
    scaled = (grad_scores * 0.125).astype(jnp.bfloat16)
    grad_queries = jnp.einsum("hqk,khe->qhe", scaled, key_rows, preferred_element_type=jnp.float32)
    grad_keys = jnp.einsum("hqk,qhe->khe", scaled, queries, preferred_element_type=jnp.float32)
    return (grad_scores.astype(jnp.bfloat16), grad_queries, grad_keys, grad_values)


def body(
    tokens,
    prev_logits,
    segment_ids,
    w_qkv,
    bias_qv,
    w_out,
    b_out,
    gain_one,
    shift_one,
    w_in,
    b_in,
    w_back,
    b_back,
    gain_two,
    shift_two,
    cotangent,
):
    rows, slots, width = tokens.shape
    heads = prev_logits.shape[1]
    count = rows * slots
    flat = tokens.reshape(count, width)
    bias_f = bias_qv.astype(jnp.float32)
    projected = jnp.einsum("td,dch->tch", flat, w_qkv, preferred_element_type=jnp.float32)
    columns = projected.shape[2]
    head_dim = columns // heads

    def shaped(array):
        return array.reshape(rows, slots, heads, head_dim)

    queries = shaped((projected[:, 0] + bias_f[0]).astype(jnp.bfloat16))
    key_rows = shaped(projected[:, 1].astype(jnp.bfloat16))
    values = shaped((projected[:, 2] + bias_f[1]).astype(jnp.bfloat16))
    raw_logits, log_total, context = lax.map(
        attend_row, (queries, key_rows, values, prev_logits, segment_ids)
    )
    context = context.reshape(count, columns)
    attended = lax.psum(jnp.dot(context, w_out, preferred_element_type=jnp.float32), "mp")
    hidden_one = flat.astype(jnp.float32) + attended + b_out.astype(jnp.float32)
    first, first_back = jax.vjp(
        normalize, hidden_one, gain_one.astype(jnp.float32), shift_one.astype(jnp.float32)
    )
    first_low = first.astype(jnp.bfloat16)
    inner = jnp.dot(first_low, w_in, preferred_element_type=jnp.float32) + b_in.astype(jnp.float32)
    active, gelu_back = jax.vjp(gelu_exact, inner)
    active_low = active.astype(jnp.bfloat16)
    branch = lax.psum(jnp.dot(active_low, w_back, preferred_element_type=jnp.float32), "mp")
    hidden_two = first + branch + b_back.astype(jnp.float32)
    output, second_back = jax.vjp(
        normalize, hidden_two, gain_two.astype(jnp.float32), shift_two.astype(jnp.float32)
    )
    grad_two, grad_gain_two, grad_shift_two = second_back(
        cotangent.reshape(count, width).astype(jnp.float32)
    )
    grad_b_back = jnp.sum(grad_two, axis=0)
    grad_two_low = grad_two.astype(jnp.bfloat16)
    grad_w_back = jnp.einsum(
        "tf,td->fd", active_low, grad_two_low, preferred_element_type=jnp.float32
    )
    grad_active = jnp.einsum("td,fd->tf", grad_two_low, w_back, preferred_element_type=jnp.float32)
    (grad_inner,) = gelu_back(grad_active)
    grad_b_in = jnp.sum(grad_inner, axis=0)
    grad_inner_low = grad_inner.astype(jnp.bfloat16)
    grad_w_in = jnp.einsum(
        "td,tf->df", first_low, grad_inner_low, preferred_element_type=jnp.float32
    )
    ffn_group = (grad_w_back, grad_b_back, grad_gain_two, grad_shift_two, grad_w_in, grad_b_in)
    grad_first = grad_two + lax.psum(
        jnp.einsum("tf,df->td", grad_inner_low, w_in, preferred_element_type=jnp.float32), "mp"
    )
    grad_one, grad_gain_one, grad_shift_one = first_back(grad_first)
    grad_b_out = jnp.sum(grad_one, axis=0)
    grad_one_low = grad_one.astype(jnp.bfloat16)
    grad_w_out = jnp.einsum("th,td->hd", context, grad_one_low, preferred_element_type=jnp.float32)
    grad_context = shaped(
        jnp.einsum("td,hd->th", grad_one_low, w_out, preferred_element_type=jnp.float32).astype(
            jnp.bfloat16
        )
    )
    grad_prev, grad_queries, grad_keys, grad_values = lax.map(
        attend_back_row,
        (queries, key_rows, values, prev_logits, segment_ids, log_total, grad_context),
    )
    grad_queries = grad_queries.reshape(count, columns)
    grad_keys = grad_keys.reshape(count, columns)
    grad_values = grad_values.reshape(count, columns)
    grad_bias_qv = jnp.stack([jnp.sum(grad_queries, axis=0), jnp.sum(grad_values, axis=0)], axis=0)
    grad_projected = jnp.stack([grad_queries, grad_keys, grad_values], axis=1).astype(jnp.bfloat16)
    grad_w_qkv = jnp.einsum("td,tch->dch", flat, grad_projected, preferred_element_type=jnp.float32)
    grad_input = grad_one + lax.psum(
        jnp.einsum("tch,dch->td", grad_projected, w_qkv, preferred_element_type=jnp.float32), "mp"
    )
    attn_group = (grad_w_qkv, grad_bias_qv, grad_w_out, grad_b_out, grad_gain_one, grad_shift_one)
    summed = lax.psum(
        (
            ffn_group[0],
            ffn_group[1],
            ffn_group[2],
            ffn_group[3],
            ffn_group[4],
            ffn_group[5],
            attn_group[0],
            attn_group[1],
            attn_group[2],
            attn_group[3],
            attn_group[4],
            attn_group[5],
        ),
        "dp",
    )
    ffn_group = tuple(summed[:6])
    attn_group = tuple(summed[6:])
    return (
        output.reshape(rows, slots, width).astype(jnp.bfloat16),
        raw_logits,
        grad_input.reshape(rows, slots, width).astype(jnp.bfloat16),
        grad_prev,
        attn_group[0],
        attn_group[1],
        attn_group[2],
        attn_group[3],
        attn_group[4],
        attn_group[5],
        ffn_group[4],
        ffn_group[5],
        ffn_group[0],
        ffn_group[1],
        ffn_group[2],
        ffn_group[3],
    )


def solution(mesh):
    in_specs = (
        P("dp", None, None),
        P("dp", "mp", None, None),
        P("dp", None),
        P(None, None, "mp"),
        P(None, "mp"),
        P("mp", None),
        P(),
        P(),
        P(),
        P(None, "mp"),
        P("mp"),
        P("mp", None),
        P(),
        P(),
        P(),
        P("dp", None, None),
    )
    out_specs = (
        P("dp", None, None),
        P("dp", "mp", None, None),
        P("dp", None, None),
        P("dp", "mp", None, None),
        P(None, None, "mp"),
        P(None, "mp"),
        P("mp", None),
        P(),
        P(),
        P(),
        P(None, "mp"),
        P("mp"),
        P("mp", None),
        P(),
        P(),
        P(),
    )
    return jax.shard_map(body, mesh=mesh, in_specs=in_specs, out_specs=out_specs, check_vma=False)
```

profile of v0, /device:TPU:0, one launch (start us, length us, event | category | flops | bytes accessed | tf_op | source)
XLA Modules:
  0.0 1059.3 jit_solution(7806687417363351328)
XLA Ops:
  7.3 4.2 fusion.117
  13.1 3.1 squeeze.38
  22.1 8.7 copy.55
  30.9 3.6 fusion.95
  34.5 3.2 broadcast.195.clone2
  37.8 61.5 %while.30 = (s32[]{:T(128)}, bf16[4,3,512,512]{3,2,1,0:T(8,128)(2,1)}, f32[4,3,512,1]{2,1,3,0:T(4,128)}, bf16[4,512,3,64]{1,3,2,0:T(8,128)(2,1)S(1)}, bf16[4,512...) while((s32[]{:T(128)}, ...), condition=%wide.region_3.4_spmd, body=%wide.region_0.3_spmd.sunk | while | flops 211647488 | bytes 36501140 | solution.py:93
  101.0 3.7 fusion.118
  105.2 122.0 %all-reduce.8.cloned.1.call-done = f32[2048,768]{1,0:T(8,128)} async-done(((f32[2048,768]{1,0:T(8,128)}), f32[2048,768]{1,0:T(8,128)}) %all-reduce.8.cloned.1.call-update) | async-done | bytes 6291472 | tf_op jit(solution)/shard_map/psum | solution.py:97
  227.3 4.6 fusion.110
  232.8 18.3 %multiply_convert_fusion.3 = (bf16[2048,768]{1,0:T(8,128)(2,1)S(1)}, f32[2048,768]{1,0:T(8,128)}, f32[2048,768]{1,0:T(8,128)}) fusion(f32[768]{0:T(1024)S(1)} %convert_element_type.122, bf16[768,768]{1,0:T(8,128)(2,1)S(1)} %copy-done, f32[2048,768]{1,0:T(8,128)S(1)} %get-tuple-element.288, f32[768]{0:T(1024)S(1)} %convert_element_type.120, ...), kind=kOutput, calls=%fused_computation.96 | convolution fusion | flops 2527592448 | bytes 23225344 | tf_op jit(solution)/shard_map/dot_general | solution.py:103
  252.7 4.5 fusion.119
  258.0 119.3 %all-reduce.10.cloned.1.call-done = f32[2048,768]{1,0:T(8,128)} async-done(((f32[2048,768]{1,0:T(8,128)}), f32[2048,768]{1,0:T(8,128)}) %all-reduce.10.cloned.1.call-update) | async-done | bytes 6291472 | tf_op jit(solution)/shard_map/psum | solution.py:106
  377.3 5.7 fusion.108
  384.9 3.0 fusion.88
  388.0 4.3 fusion.107
  392.4 5.6 fusion.114
  399.6 4.5 fusion.99
  404.1 11.1 %all-reduce.14.cloned.1.call-start = ((), (), s32[]{:S(2)}) async-start(), calls=%async_computation.3 | async-start | bytes 12582912 | tf_op jit(solution)/shard_map/psum | solution.py:149
  415.3 108.8 %all-reduce.12.cloned.1.call-done = f32[2048,768]{1,0:T(8,128)} async-done(((f32[2048,768]{1,0:T(8,128)}), f32[2048,768]{1,0:T(8,128)}) %all-reduce.12.cloned.1.call-update) | async-done | bytes 6291472 | tf_op jit(solution)/shard_map/psum | solution.py:127
  524.1 8.1 multiply_reduce_fusion.1
  532.3 4.2 fusion.106
  541.2 3.2 broadcast.195.clone
  544.4 125.9 %while.31 = (s32[]{:T(128)}, bf16[4,3,512,512]{3,2,1,0:T(8,128)(2,1)}, f32[4,512,3,64]{1,3,2,0:T(8,128)}, bf16[4,512,3,64]{1,3,2,0:T(8,128)(2,1)}, f32[4,512,3,6...) while((s32[]{:T(128)}, ...), condition=%wide.region_17.18_spmd, body=%wide.region_15.17_spmd.sunk | while | flops 721164800 | bytes 74679016 | solution.py:139
  551.8 5.3 convert_bitcast_fusion.3
  558.8 3.3 fusion.180
  562.1 5.8 fusion.182
  567.9 6.7 fusion.181
  583.3 5.3 convert_bitcast_fusion.3
  590.3 3.3 fusion.180
  593.6 5.8 fusion.182
  599.3 6.7 fusion.181
  614.7 5.3 convert_bitcast_fusion.3
  621.8 3.3 fusion.180
  625.1 5.8 fusion.182
  630.8 6.7 fusion.181
  646.2 5.4 convert_bitcast_fusion.3
  653.3 3.3 fusion.180
  656.6 5.8 fusion.182
  662.4 6.7 fusion.181
  681.0 5.8 convolution_bitcast_fusion.2
  687.6 8.0 fusion.103
  695.6 7.5 fusion.97
  706.1 3.2 convolution_bitcast_fusion.3
  712.0 94.9 %all-reduce.14.cloned.1.call-done = f32[2048,768]{1,0:T(8,128)} async-done(((f32[2048,768]{1,0:T(8,128)}), f32[2048,768]{1,0:T(8,128)}) %all-reduce.14.cloned.1.call-update) | async-done | bytes 6291472 | tf_op jit(solution)/shard_map/psum | solution.py:149
  806.8 6.8 add_reduce_fusion.1
  813.6 40.0 %all-reduce = (f32[2,192]{1,0:T(2,128)}, f32[768]{0:T(1024)}, f32[768]{0:T(1024)}, f32[768]{0:T(1024)}, f32[768]{0:T(1024)}, /*index=5*/f32[768]{0:T(1024)}, f32[768]{0:T(1024)}, f32[768]{0:T(1024)}) all-reduce(f32[2,192]{1,0:T(2,128)S(1)} %pad_maximum_fusion, ...), channel_id=1, replica_groups=mesh['dp'=8,'mp'=4] {'dp'}, use_global_device_ids=true, to_apply=%region_22.23 | all-reduce | flops 5760 | bytes 46080 | tf_op jit(solution)/shard_map/psum | solution.py:153
  853.6 191.1 %all-reduce.16.cloned.1.call-done = (f32[768,3,192]{0,2,1:T(8,128)}, f32[192,768]{1,0:T(8,128)}, f32[768,768]{1,0:T(8,128)}, f32[768,768]{1,0:T(8,128)}) async-done(((f32[768,3,192]{0,2,1:T(8,128)}, f32[192,768]{1,0:T(8,128)}, f32[768,768]{1,0:T(8,128)}, f32[768,768]{1,0:T(8,128)}), (f32[768,3,192]{0,2,1:T(8,128)}, f32[192,768]{1,0:T(8,128)}, f32[768,768]{1,0:T(8,128)}, ...) | async-done | bytes 7077904 | tf_op jit(solution)/shard_map/psum | solution.py:153
  1044.7 2.9 copy.130
  (245 shorter events, 145.2 us)
Async XLA Ops:
  7.2 225.6 %copy-start = (bf16[768,768]{1,0:T(8,128)(2,1)S(1)}, bf16[768,768]{1,0:T(8,128)(2,1)}, u32[]{:S(2)}) copy-start(bf16[768,768]{1,0:T(8,128)(2,1)} %param.29) | copy-start | bytes 3538948
  7.2 220.1 %all-reduce.8.cloned.1.call-start = ((), (), s32[]{:S(2)}) async-start(), calls=%async_computation | async-start | bytes 12582912 | tf_op jit(solution)/shard_map/psum | solution.py:97
  22.1 8.7 copy-start.10
  30.9 6.9 copy-start.15
  37.8 63.3 %copy-start.14 = (bf16[192,768]{1,0:T(8,128)(2,1)S(1)}, bf16[192,768]{1,0:T(8,128)(2,1)}, u32[]{:S(2)}) copy-start(bf16[192,768]{1,0:T(8,128)(2,1)} %param.25) | copy-start | bytes 884740
  101.0 4.1 copy-start.28
  101.0 4.1 copy-start.29
  101.0 4.2 copy-start.30
  101.0 4.2 copy-start.31
  104.8 272.5 %all-reduce.10.cloned.1.call-start = ((), (), s32[]{:S(2)}) async-start(), calls=%async_computation.1 | async-start | bytes 12582912 | tf_op jit(solution)/shard_map/psum | solution.py:106
  105.2 427.1 %copy-start.20 = (f32[768]{0:T(1024)}, f32[768]{0:T(1024)S(1)}, u32[]{:S(2)}) copy-start(f32[768]{0:T(1024)S(1)} %convert_element_type.119) | copy-start | bytes 9220
  105.2 272.1 %copy-start.25 = (f32[768]{0:T(1024)}, f32[768]{0:T(1024)S(1)}, u32[]{:S(2)}) copy-start(f32[768]{0:T(1024)S(1)} %convert_element_type.120) | copy-start | bytes 9220
  231.9 19.2 %copy-start.4 = (f32[2048,768]{1,0:T(8,128)}, f32[2048,768]{1,0:T(8,128)S(1)}, u32[]{:S(2)}) copy-start(f32[2048,768]{1,0:T(8,128)S(1)} %get-tuple-element.288) | copy-start | bytes 18874372
  232.8 20.0 %copy-start.36 = (bf16[768,768]{1,0:T(8,128)(2,1)S(1)}, bf16[768,768]{1,0:T(8,128)(2,1)}, u32[]{:S(2)}) copy-start(bf16[768,768]{1,0:T(8,128)(2,1)} %param.31) | copy-start | bytes 3538948
  257.3 266.8 %all-reduce.12.cloned.1.call-start = ((), (), s32[]{:S(2)}) async-start(), calls=%async_computation.2 | async-start | bytes 12582912 | tf_op jit(solution)/shard_map/psum | solution.py:127
  383.0 1.9 copy-start.6
  384.9 7.4 slice-start.2
  384.9 7.4 slice-start.4
  387.9 4.4 copy-start.37
  387.9 4.4 slice-start.3
  388.0 4.4 slice-start.5
  392.3 5.7 copy-start.7
  392.3 131.8 %copy-start.22 = (f32[2048]{0:T(1024)}, f32[2048]{0:T(1024)S(1)}, u32[]{:S(2)}) copy-start(f32[2048]{0:T(1024)S(1)} %negate_multiply_fusion.2) | copy-start | bytes 24580
  404.1 402.7 %all-reduce.14.cloned.1.call-start = ((), (), s32[]{:S(2)}) async-start(), calls=%async_computation.3 | async-start | bytes 12582912 | tf_op jit(solution)/shard_map/psum | solution.py:149
  536.5 2.6 copy-start.5
  548.7 1.8 copy-start.3
  551.8 10.3 copy-start.16
  567.9 8.0 copy-start.17
  583.3 10.3 copy-start.16
  599.3 8.0 copy-start.17
  614.7 10.3 copy-start.16
  630.8 8.0 copy-start.17
  646.2 10.4 copy-start.16
  662.4 8.0 copy-start.17
  686.9 8.7 copy-start.21
  686.9 8.7 copy-start.26
  686.9 357.8 %all-reduce.16.cloned.1.call-start = ((), (), s32[]{:S(2)}) async-start(), calls=%async_computation.4 | async-start | bytes 14155776 | tf_op jit(solution)/shard_map/psum | solution.py:153
  687.5 8.1 copy-start.40
  687.6 15.6 %slice-start = ((s8[6291456]{0:T(1024)(128)(4,1)}), s8[4194304]{0:T(1024)(128)(4,1)S(1)}, s32[]{:S(2)}) async-start(s8[6291456]{0:T(1024)(128)(4,1)} %bitcast.191), calls=%async_computation.5 | async-start | bytes 8388608
  695.6 7.5 slice-start.1
  695.6 7.5 copy-start.9
  703.2 1.9 copy-start.11
  703.2 2.9 copy-start.19
  711.9 101.7 %copy-start.24 = (f32[768]{0:T(1024)S(1)}, f32[768]{0:T(1024)}, u32[]{:S(2)}) copy-start(f32[768]{0:T(1024)} %get-tuple-element.213) | copy-start | bytes 9220
  711.9 101.7 %copy-start.27 = (f32[768]{0:T(1024)S(1)}, f32[768]{0:T(1024)}, u32[]{:S(2)}) copy-start(f32[768]{0:T(1024)} %get-tuple-element.304) | copy-start | bytes 9220
  1044.7 4.9 copy-start.13
  1044.7 6.3 copy-start.12
  1044.7 7.7 copy-start.1
  (16 other events, 21.8 us)
Sparse Core Ops, SparseCore 0:
  104.9 122.2 all-reduce.7
  257.4 119.7 all-reduce.9
  404.3 119.7 all-reduce.11
  687.0 119.7 all-reduce.13
  812.2 232.3 all-reduce.15
where the time goes:
time: 1070 us; the launch traced here: 1060 us
  waiting for transfers between devices  636 us (59%)
  matrix products  189 us (18%)
  local copies, waits for them, and re-layouts  101 us (9%)
  other arithmetic  66.2 us (6%)
  blocking collectives  40 us (4%)
  between operations  14.8 us (1%)
  starting transfers between devices  11.7 us (1%)
    psum x1, waiting for transfers between devices, body(): lax.psum((ffn_group[0], ffn_group[1], ffn_group[2], ffn_group[3], ffn_gro...  191 us
    psum x1, waiting for transfers between devices, body(): lax.psum(jnp.dot(context, w_out, preferred_element_type=jnp.float32), 'mp')  122 us
    psum x1, waiting for transfers between devices, body(): lax.psum(jnp.dot(active_low, w_back, preferred_element_type=jnp.float32),...  119 us
    psum x1, waiting for transfers between devices, body(): lax.psum(jnp.einsum('tf,df->td', grad_inner_low, w_in, preferred_element_...  109 us
    psum x1, waiting for transfers between devices, body(): lax.psum(jnp.einsum('tch,dch->td', grad_projected, w_qkv, preferred_eleme...  94.9 us
    psum x1, blocking collectives, body(): lax.psum((ffn_group[0], ffn_group[1], ffn_group[2], ffn_group[3], ffn_gro...  40 us
    dynamic_update_slice x16, local copies, waits for them, and re-layouts, body(): lax.map(attend_row, (queries, key_rows, values, prev_logits, segment_ids))  32.8 us
    dot_general x4, matrix products, attend_back_row(): jnp.einsum('hqk,khe->qhe', scaled, key_rows, preferred_element_type=jnp.f...  27 us
  transfers between devices with their start and end apart: 5, of which 5 were waited for; matrix products, arithmetic and copies ran while one was open for 3% of the time, Pallas kernels for 0%

commit v1 on v0

--- a/solution.py
+++ b/solution.py
@@ -124,8 +124,11 @@
         "td,tf->df", first_low, grad_inner_low, preferred_element_type=jnp.float32
     )
     ffn_group = (grad_w_back, grad_b_back, grad_gain_two, grad_shift_two, grad_w_in, grad_b_in)
-    grad_first = grad_two + lax.psum(
-        jnp.einsum("tf,df->td", grad_inner_low, w_in, preferred_element_type=jnp.float32), "mp"
+    grad_first = grad_two + jnp.sum(
+        lax.all_gather(
+            jnp.einsum("tf,df->td", grad_inner_low, w_in, preferred_element_type=jnp.float32), "mp"
+        ),
+        axis=0,
     )
     grad_one, grad_gain_one, grad_shift_one = first_back(grad_first)
     grad_b_out = jnp.sum(grad_one, axis=0)

time: 1070 us -> 1130 us (1.056)
  waiting for transfers between devices: 636 us -> 682 us
  matrix products: 189 us -> 206 us
    all_gather x0 -> x1, waiting for transfers between devices: none -> 155 us  [body(): lax.all_gather(jnp.einsum('tf,df->td', grad_inner_low, w_in, preferred_el...]
    psum x1 -> x0, waiting for transfers between devices: 109 us -> none  [body(): lax.psum(jnp.einsum('tf,df->td', grad_inner_low, w_in, preferred_element_...]
    reduce_sum x0 -> x1, other arithmetic: none -> 12.7 us  [body(): jnp.sum(lax.all_gather(jnp.einsum('tf,df->td', grad_inner_low, w_in, pref...]
where the time goes in v1:
time: 1130 us; the launch traced here: 1120 us
  waiting for transfers between devices  682 us (60%)
  matrix products  206 us (18%)
  local copies, waits for them, and re-layouts  94.8 us (8%)
  other arithmetic  77.1 us (7%)
  blocking collectives  40 us (4%)
  between operations  14.5 us (1%)
    psum x1, waiting for transfers between devices, body(): lax.psum((ffn_group[0], ffn_group[1], ffn_group[2], ffn_group[3], ffn_gro...  191 us
    all_gather x1, waiting for transfers between devices, body(): lax.all_gather(jnp.einsum('tf,df->td', grad_inner_low, w_in, preferred_el...  155 us
    psum x1, waiting for transfers between devices, body(): lax.psum(jnp.dot(context, w_out, preferred_element_type=jnp.float32), 'mp')  122 us
    psum x1, waiting for transfers between devices, body(): lax.psum(jnp.dot(active_low, w_back, preferred_element_type=jnp.float32),...  119 us
    psum x1, waiting for transfers between devices, body(): lax.psum(jnp.einsum('tch,dch->td', grad_projected, w_qkv, preferred_eleme...  94.6 us
    psum x1, blocking collectives, body(): lax.psum((ffn_group[0], ffn_group[1], ffn_group[2], ffn_group[3], ffn_gro...  40 us
    dynamic_update_slice x16, local copies, waits for them, and re-layouts, body(): lax.map(attend_row, (queries, key_rows, values, prev_logits, segment_ids))  33.1 us
    dot_general x8, matrix products, row_scores(): jnp.einsum('qhe,khe->hqk', queries, key_rows, preferred_element_type=jnp....  26.9 us
  transfers between devices with their start and end apart: 5, of which 5 were waited for; matrix products, arithmetic and copies ran while one was open for 3% of the time, Pallas kernels for 0%

profile of v1, /device:TPU:0, one launch (start us, length us, event | category | flops | bytes accessed | tf_op | source)
XLA Modules:
  0.0 1116.1 jit_solution(15620538389329979642)
XLA Ops:
  7.3 4.2 fusion.117
  20.1 8.6 copy.55
  28.7 3.8 fusion.95
  32.6 3.2 broadcast.195.clone2
  35.8 63.8 %while.30 = (s32[]{:T(128)}, bf16[4,3,512,512]{3,2,1,0:T(8,128)(2,1)}, f32[4,3,512,1]{2,1,3,0:T(4,128)}, bf16[4,512,3,64]{1,3,2,0:T(8,128)(2,1)}, bf16[4,512,3,6...) while((s32[]{:T(128)}, ...), condition=%wide.region_3.4_spmd, body=%wide.region_0.3_spmd.sunk | while | flops 211647488 | bytes 36501140 | solution.py:93
  102.7 3.7 fusion.118
  106.8 122.1 %all-reduce.7.cloned.1.call-done = f32[2048,768]{1,0:T(8,128)} async-done(((f32[2048,768]{1,0:T(8,128)}), f32[2048,768]{1,0:T(8,128)}) %all-reduce.7.cloned.1.call-update) | async-done | bytes 6291472 | tf_op jit(solution)/shard_map/psum | solution.py:97
  228.9 4.6 fusion.110
  234.5 18.3 %multiply_convert_fusion.3 = (bf16[2048,768]{1,0:T(8,128)(2,1)S(1)}, f32[2048,768]{1,0:T(8,128)}, f32[2048,768]{1,0:T(8,128)}) fusion(f32[768]{0:T(1024)S(1)} %convert_element_type.122, bf16[768,768]{1,0:T(8,128)(2,1)S(1)} %copy-done, f32[2048,768]{1,0:T(8,128)S(1)} %get-tuple-element.288, f32[768]{0:T(1024)S(1)} %convert_element_type.120, ...), kind=kOutput, calls=%fused_computation.96 | convolution fusion | flops 2527592448 | bytes 23225344 | tf_op jit(solution)/shard_map/dot_general | solution.py:103
  254.5 4.5 fusion.119
  259.7 119.3 %all-reduce.9.cloned.1.call-done = f32[2048,768]{1,0:T(8,128)} async-done(((f32[2048,768]{1,0:T(8,128)}), f32[2048,768]{1,0:T(8,128)}) %all-reduce.9.cloned.1.call-update) | async-done | bytes 6291472 | tf_op jit(solution)/shard_map/psum | solution.py:106
  378.9 5.7 fusion.108
  389.6 4.3 fusion.107
  394.0 5.6 fusion.114
  401.3 4.5 fusion.99
  406.1 154.9 %all-gather.3.cloned.1.call-done = f32[8192,768]{1,0:T(8,128)} async-done(((f32[2048,768]{1,0:T(8,128)}), f32[8192,768]{1,0:T(8,128)}) %all-gather.3.cloned.1.call-update) | async-done | bytes 25165840 | tf_op jit(solution)/shard_map/all_gather | solution.py:128
  560.9 12.7 %reduce_sum.186 = f32[2048,768]{1,0:T(8,128)} reduce(f32[4,2048,768]{2,1,0:T(8,128)} %bitcast.194, f32[]{:T(128)} %constant.64.clone.1), dimensions={0}, to_apply=%region_12.13 | reduce | flops 4718592 | bytes 31457284 | tf_op jit(solution)/shard_map/reduce_sum | solution.py:127
  573.6 8.2 multiply_reduce_fusion.1
  581.8 4.2 fusion.106
  590.8 3.2 broadcast.195.clone
  594.0 132.8 %while.31 = (s32[]{:T(128)}, bf16[4,3,512,512]{3,2,1,0:T(8,128)(2,1)}, f32[4,512,3,64]{1,3,2,0:T(8,128)}, bf16[4,512,3,64]{1,3,2,0:T(8,128)(2,1)}, f32[4,512,3,6...) while((s32[]{:T(128)}, ...), condition=%wide.region_17.18_spmd, body=%wide.region_15.17_spmd.sunk | while | flops 721164800 | bytes 62096072 | solution.py:142
  595.7 4.3 fusion.179
  600.0 5.1 convert_bitcast_fusion.3
  611.3 6.5 fusion.181
  617.8 5.7 fusion.182
  623.6 3.5 fusion.183
  628.8 4.3 fusion.179
  633.1 5.1 convert_bitcast_fusion.3
  644.4 6.6 fusion.181
  650.9 5.7 fusion.182
  656.7 3.5 fusion.183
  661.9 4.3 fusion.179
  666.2 5.1 convert_bitcast_fusion.3
  677.5 6.6 fusion.181
  684.0 5.7 fusion.182
  689.8 3.5 fusion.183
  695.0 4.3 fusion.179
  699.3 5.1 convert_bitcast_fusion.3
  710.6 6.6 fusion.181
  717.2 5.8 fusion.182
  723.0 3.5 fusion.183
  736.8 7.2 convolution_bitcast_fusion.2
  744.7 8.1 fusion.103
  752.9 7.5 fusion.97
  769.2 94.6 %all-reduce.11.cloned.1.call-done = f32[2048,768]{1,0:T(8,128)} async-done(((f32[2048,768]{1,0:T(8,128)}), f32[2048,768]{1,0:T(8,128)}) %all-reduce.11.cloned.1.call-update) | async-done | bytes 6291472 | tf_op jit(solution)/shard_map/psum | solution.py:152
  863.8 6.8 add_reduce_fusion.1
  870.6 40.0 %all-reduce = (f32[2,192]{1,0:T(2,128)}, f32[768]{0:T(1024)}, f32[768]{0:T(1024)}, f32[768]{0:T(1024)}, f32[768]{0:T(1024)}, /*index=5*/f32[768]{0:T(1024)}, f32[768]{0:T(1024)}, f32[768]{0:T(1024)}) all-reduce(f32[2,192]{1,0:T(2,128)S(1)} %pad_maximum_fusion, ...), channel_id=1, replica_groups=mesh['dp'=8,'mp'=4] {'dp'}, use_global_device_ids=true, to_apply=%region_22.23 | all-reduce | flops 5760 | bytes 46080 | tf_op jit(solution)/shard_map/psum | solution.py:156
  910.6 191.1 %all-reduce.13.cloned.1.call-done = (f32[768,3,192]{0,2,1:T(8,128)}, f32[192,768]{1,0:T(8,128)}, f32[768,768]{1,0:T(8,128)}, f32[768,768]{1,0:T(8,128)}) async-done(((f32[768,3,192]{0,2,1:T(8,128)}, f32[192,768]{1,0:T(8,128)}, f32[768,768]{1,0:T(8,128)}, f32[768,768]{1,0:T(8,128)}), (f32[768,3,192]{0,2,1:T(8,128)}, f32[192,768]{1,0:T(8,128)}, f32[768,768]{1,0:T(8,128)}, ...) | async-done | bytes 7077904 | tf_op jit(solution)/shard_map/psum | solution.py:156
  (234 shorter events, 149.1 us)
Async XLA Ops:
  7.2 227.3 %copy-start = (bf16[768,768]{1,0:T(8,128)(2,1)S(1)}, bf16[768,768]{1,0:T(8,128)(2,1)}, u32[]{:S(2)}) copy-start(bf16[768,768]{1,0:T(8,128)(2,1)} %param.29) | copy-start | bytes 3538948
  7.2 221.7 %all-reduce.7.cloned.1.call-start = ((), (), s32[]{:S(2)}) async-start(), calls=%async_computation | async-start | bytes 12582912 | tf_op jit(solution)/shard_map/psum | solution.py:97
  11.5 4.6 copy-start.33
  35.8 66.9 %copy-start.14 = (bf16[192,768]{1,0:T(8,128)(2,1)S(1)}, bf16[192,768]{1,0:T(8,128)(2,1)}, u32[]{:S(2)}) copy-start(bf16[192,768]{1,0:T(8,128)(2,1)} %param.25) | copy-start | bytes 884740
  99.6 6.9 copy-start.5
  102.7 4.0 copy-start.26
  102.7 4.0 copy-start.27
  102.7 4.1 copy-start.28
  102.7 4.1 copy-start.29
  106.5 272.4 %all-reduce.9.cloned.1.call-start = ((), (), s32[]{:S(2)}) async-start(), calls=%async_computation.1 | async-start | bytes 12582912 | tf_op jit(solution)/shard_map/psum | solution.py:106
  106.8 272.2 %copy-start.23 = (f32[768]{0:T(1024)}, f32[768]{0:T(1024)S(1)}, u32[]{:S(2)}) copy-start(f32[768]{0:T(1024)S(1)} %convert_element_type.120) | copy-start | bytes 9220
  106.8 475.0 %copy-start.18 = (f32[768]{0:T(1024)}, f32[768]{0:T(1024)S(1)}, u32[]{:S(2)}) copy-start(f32[768]{0:T(1024)S(1)} %convert_element_type.119) | copy-start | bytes 9220
  233.5 19.2 %copy-start.3 = (f32[2048,768]{1,0:T(8,128)}, f32[2048,768]{1,0:T(8,128)S(1)}, u32[]{:S(2)}) copy-start(f32[2048,768]{1,0:T(8,128)S(1)} %get-tuple-element.288) | copy-start | bytes 18874372
  234.4 20.1 %copy-start.34 = (bf16[768,768]{1,0:T(8,128)(2,1)S(1)}, bf16[768,768]{1,0:T(8,128)(2,1)}, u32[]{:S(2)}) copy-start(bf16[768,768]{1,0:T(8,128)(2,1)} %param.31) | copy-start | bytes 3538948
  252.8 1.7 copy-start.35
  259.0 301.9 %all-gather.3.cloned.1.call-start = ((), (), s32[]{:S(2)}) async-start(), calls=%async_computation.3 | async-start | bytes 31457280 | tf_op jit(solution)/shard_map/all_gather | solution.py:128
  384.6 1.9 copy-start.6
  386.5 7.4 slice-start.2
  386.5 7.4 slice-start.4
  389.6 4.4 slice-start.3
  389.6 4.4 slice-start.5
  393.9 5.6 copy-start.7
  394.0 179.7 %copy-start.20 = (f32[2048]{0:T(1024)}, f32[2048]{0:T(1024)S(1)}, u32[]{:S(2)}) copy-start(f32[2048]{0:T(1024)S(1)} %negate_multiply_fusion.2) | copy-start | bytes 24580
  405.8 458.0 %all-reduce.11.cloned.1.call-start = ((), (), s32[]{:S(2)}) async-start(), calls=%async_computation.2 | async-start | bytes 12582912 | tf_op jit(solution)/shard_map/psum | solution.py:152
  586.1 2.7 copy-start.4
  605.1 12.8 %copy-start.15 = (bf16[4,512,3,64]{1,3,2,0:T(8,128)(2,1)S(1)}, bf16[4,512,3,64]{1,3,2,0:T(8,128)(2,1)}, u32[]{:S(2)}) copy-start(bf16[4,512,3,64]{1,3,2,0:T(8,128)(2,1)} %get-tuple-element.504) | copy-start | bytes 2359300 | tf_op jit(solution)/shard_map/while
  623.6 3.5 copy-start.16
  638.2 12.8 %copy-start.15 = (bf16[4,512,3,64]{1,3,2,0:T(8,128)(2,1)S(1)}, bf16[4,512,3,64]{1,3,2,0:T(8,128)(2,1)}, u32[]{:S(2)}) copy-start(bf16[4,512,3,64]{1,3,2,0:T(8,128)(2,1)} %get-tuple-element.504) | copy-start | bytes 2359300 | tf_op jit(solution)/shard_map/while
  656.7 3.5 copy-start.16
  671.2 12.8 %copy-start.15 = (bf16[4,512,3,64]{1,3,2,0:T(8,128)(2,1)S(1)}, bf16[4,512,3,64]{1,3,2,0:T(8,128)(2,1)}, u32[]{:S(2)}) copy-start(bf16[4,512,3,64]{1,3,2,0:T(8,128)(2,1)} %get-tuple-element.504) | copy-start | bytes 2359300 | tf_op jit(solution)/shard_map/while
  689.8 3.5 copy-start.16
  704.4 12.8 %copy-start.15 = (bf16[4,512,3,64]{1,3,2,0:T(8,128)(2,1)S(1)}, bf16[4,512,3,64]{1,3,2,0:T(8,128)(2,1)}, u32[]{:S(2)}) copy-start(bf16[4,512,3,64]{1,3,2,0:T(8,128)(2,1)} %get-tuple-element.504) | copy-start | bytes 2359300 | tf_op jit(solution)/shard_map/while
  723.0 3.5 copy-start.16
  726.9 6.7 copy-start.13
  744.1 8.8 copy-start.19
  744.1 8.8 copy-start.24
  744.1 357.6 %all-reduce.13.cloned.1.call-start = ((), (), s32[]{:S(2)}) async-start(), calls=%async_computation.4 | async-start | bytes 14155776 | tf_op jit(solution)/shard_map/psum | solution.py:156
  744.7 8.1 copy-start.37
  744.7 15.6 %slice-start = ((s8[6291456]{0:T(1024)(128)(4,1)}), s8[4194304]{0:T(1024)(128)(4,1)S(1)}, s32[]{:S(2)}) async-start(s8[6291456]{0:T(1024)(128)(4,1)} %bitcast.192), calls=%async_computation.5 | async-start | bytes 8388608
  752.8 7.5 slice-start.1
  752.9 7.5 copy-start.9
  760.4 1.9 copy-start.10
  760.4 2.9 copy-start.17
  769.2 101.4 %copy-start.22 = (f32[768]{0:T(1024)S(1)}, f32[768]{0:T(1024)}, u32[]{:S(2)}) copy-start(f32[768]{0:T(1024)} %get-tuple-element.213) | copy-start | bytes 9220
  769.2 101.4 %copy-start.25 = (f32[768]{0:T(1024)S(1)}, f32[768]{0:T(1024)}, u32[]{:S(2)}) copy-start(f32[768]{0:T(1024)} %get-tuple-element.304) | copy-start | bytes 9220
  1101.7 4.9 copy-start.12
  1101.7 6.3 copy-start.11
  1101.7 7.7 copy-start.1
  (10 other events, 12.0 us)
Sparse Core Ops, SparseCore 0:
  106.6 122.2 all-reduce.6
  259.1 119.7 all-reduce.8
  405.9 154.9 all-gather.2
  744.2 119.5 all-reduce.10
  869.2 232.3 all-reduce.12
